TPU v7x, 256 devices: a whole 4x4x8 slice. The times are simulated.
256 devices in a mesh: dp: 8 (over x, core), expert: 32 (over y, z).
Axes of the slice: x: 4, y: 4, z: 8, core: 2. Of those that a mesh axis runs over, the one named last changes fastest.
Arguments:
- tokens: bfloat16 [12288, 2048], P(('dp', 'expert')), may hold values from -6 to 6
- routes: int32 [12288, 6], P(('dp', 'expert')), may hold values from 0 to 31, all different within a row; in each aligned block of 48 rows (0 to 47, 48 to 95, ...) at most 12 rows name the same one
- gates: float32 [12288, 6], P(('dp', 'expert')), may hold values from 0.02 to 0.5
- cotangent: bfloat16 [12288, 2048], P(('dp', 'expert')), may hold values from -6 to 6
- swap_flag: int32 [32], replicated, may hold values from 0 to 1, as said below
- w_up: bfloat16 [32, 2048, 1408], P('expert', 'dp'), may hold values from -0.125 to 0.125
- w_down: bfloat16 [32, 1408, 2048], P('expert', 'dp'), may hold values from -0.15625 to 0.15625
- m_up: bfloat16 [32, 2048, 1408], P('expert', 'dp'), may hold values from -12 to 12
- v_up: bfloat16 [32, 2048, 1408], P('expert', 'dp'), may hold values from 1 to 50
- m_down: bfloat16 [32, 1408, 2048], P('expert', 'dp'), may hold values from -12 to 12
- v_down: bfloat16 [32, 1408, 2048], P('expert', 'dp'), may hold values from 1 to 50
Outputs:
- mixed: bfloat16 [12288, 2048], P(('dp', 'expert'))
- input_grad: bfloat16 [12288, 2048], P(('dp', 'expert'))
- new_w_up: bfloat16 [32, 2048, 1408], P('expert', 'dp')
- new_w_down: bfloat16 [32, 1408, 2048], P('expert', 'dp')
- new_m_up: bfloat16 [32, 2048, 1408], P('expert', 'dp')
- new_v_up: bfloat16 [32, 2048, 1408], P('expert', 'dp')
- new_m_down: bfloat16 [32, 1408, 2048], P('expert', 'dp')
- new_v_down: bfloat16 [32, 1408, 2048], P('expert', 'dp')
Inputs may be any that keep to these rules, and one draw needn't show every extreme that they name: `routes`: in each aligned block of 48 rows (the tokens of one device) no expert is chosen by more than 12 rows, a bound that some block reaches; the 6 experts of a row differ. swap_flag[e] == swap_flag[e xor 1] for every e; the pairs of experts 0 and 2 * (8) trade places in every draw, and some other pair stays.
All inputs are finite; a program needn't handle non-finite values.
Results may differ from a plain program's by a relative error of at most 0.015.
Values may be sent and summed in bfloat16 or wider, within the bound.
No kernel may reach another device: no remote copies, remote signals or barrier semaphores. Data moves between devices by JAX's collectives and lax.ppermute only.
A program may use at most 128 MiB of HBM per device.

v0:
```python
import jax
import jax.numpy as jnp
from jax import lax
from jax.sharding import PartitionSpec as P

ADAM_STEP = 10
beta_one = 0.9
beta_two = 0.95
learn_rate = 0.001
adam_eps = 1e-08


def partner(value, axis, distance):
    mask = 2**distance
    pairs = [(source, source ^ mask) for source in range(lax.axis_size(axis))]
    return lax.ppermute(value, axis, pairs)


def silu_slope(value):
    sigma = jax.nn.sigmoid(value)
    return sigma * (1.0 + value * (1.0 - sigma))


def adam_update(weight, first_moment, second_moment, gradient):
    first_new = beta_one * first_moment.astype(jnp.float32) + (1.0 - beta_one) * gradient
    second_new = (
        beta_two * second_moment.astype(jnp.float32) + (1.0 - beta_two) * gradient * gradient
    )
    correct_one = 1.0 - beta_one**ADAM_STEP
    correct_two = 1.0 - beta_two**ADAM_STEP
    weight_new = weight.astype(jnp.float32) - learn_rate * (first_new / correct_one) / (
        jnp.sqrt(second_new / correct_two) + adam_eps
    )
    return (
        weight_new.astype(jnp.bfloat16),
        first_new.astype(jnp.bfloat16),
        second_new.astype(jnp.bfloat16),
    )


def contract_rows(left, right):
    return lax.dot_general(
        left, right, (((0,), (0,)), ((), ())), preferred_element_type=jnp.float32
    )


def contract_cols(left, right):
    return lax.dot_general(
        left, right, (((1,), (1,)), ((), ())), preferred_element_type=jnp.float32
    )


def stack_state(members):
    return jnp.stack([member.reshape(-1) for member in members])


def unstack_state(stacked, member_shapes):
    return tuple(
        (stacked[number].reshape(member_shape) for number, member_shape in enumerate(member_shapes))
    )


def body(tokens, routes, gates, cotangent, swap_flag, w_up, w_down, m_up, v_up, m_down, v_down):
    experts = lax.axis_size("expert")
    my_slot = lax.axis_index("expert")
    tok_count, model_width = tokens.shape
    chosen = routes.shape[1]
    pair_count = tok_count * chosen
    capacity = pair_count * 4 // (3 * experts)
    row_total = experts * capacity
    my_flag = swap_flag[my_slot]
    swapped = my_flag == 1
    w_up_in = partner(w_up, "expert", 0)
    w_down_in = partner(w_down, "expert", 0)
    up_moments = partner(jnp.concatenate([m_up, v_up], axis=0), "expert", 0)
    down_moments = partner(jnp.concatenate([m_down, v_down], axis=0), "expert", 0)
    w_up_use = jnp.where(swapped, w_up_in, w_up)
    w_down_use = jnp.where(swapped, w_down_in, w_down)
    m_up_use = jnp.where(swapped, up_moments[0:1], m_up)
    v_up_use = jnp.where(swapped, up_moments[1:2], v_up)
    m_down_use = jnp.where(swapped, down_moments[0:1], m_down)
    v_down_use = jnp.where(swapped, down_moments[1:2], v_down)
    flat_routes = routes.reshape(pair_count)
    dest_routes = jnp.bitwise_xor(flat_routes, swap_flag[flat_routes])
    one_hot = (dest_routes[:, None] == jnp.arange(experts, dtype=jnp.int32)[None, :]).astype(
        jnp.int32
    )
    position = jnp.sum(jnp.cumsum(one_hot, axis=0) * one_hot, axis=1) - 1
    slot_index = dest_routes * capacity + position
    source = (
        jnp.full((row_total,), -1, jnp.int32)
        .at[slot_index]
        .set(jnp.arange(pair_count, dtype=jnp.int32))
    )
    is_live = source >= 0
    safe_source = jnp.maximum(source, 0)
    token_ids = safe_source // chosen
    send_tokens = jnp.where(
        is_live[:, None], tokens[token_ids], jnp.zeros((), jnp.bfloat16)
    ).reshape(experts, capacity, model_width)
    live_gates = jnp.where(is_live, gates.reshape(pair_count)[safe_source], 0.0)
    send_grads = (
        (live_gates[:, None] * cotangent[token_ids].astype(jnp.float32))
        .astype(jnp.bfloat16)
        .reshape(experts, capacity, model_width)
    )
    up_full = lax.all_gather(w_up_use, "dp", axis=1, tiled=True)[0]
    down_full = lax.all_gather(w_down_use, "dp", axis=1, tiled=True)[0]
    got_both = lax.all_to_all(
        jnp.concatenate([send_tokens, send_grads], axis=1),
        "expert",
        split_axis=0,
        concat_axis=0,
        tiled=True,
    )
    expert_rows = got_both[:, :capacity].reshape(row_total, model_width)
    grad_rows = got_both[:, capacity:].reshape(row_total, model_width)
    up_act = jnp.dot(expert_rows, up_full, preferred_element_type=jnp.float32)
    hidden = jax.nn.silu(up_act).astype(jnp.bfloat16)
    expert_out = jnp.dot(hidden, down_full, preferred_element_type=jnp.float32).astype(jnp.bfloat16)
    returned = lax.all_to_all(
        expert_out.reshape(experts, capacity, model_width),
        "expert",
        split_axis=0,
        concat_axis=0,
        tiled=True,
    )
    picked = returned.reshape(row_total, model_width)[slot_index].reshape(
        tok_count, chosen, model_width
    )
    mixed = jnp.sum(gates[:, :, None] * picked.astype(jnp.float32), axis=1).astype(jnp.bfloat16)
    hidden_grad = contract_cols(grad_rows, down_full)
    up_grad = (hidden_grad * silu_slope(up_act)).astype(jnp.bfloat16)
    input_part = contract_cols(up_grad, up_full).astype(jnp.bfloat16)
    back_grads = lax.all_to_all(
        input_part.reshape(experts, capacity, model_width),
        "expert",
        split_axis=0,
        concat_axis=0,
        tiled=True,
    )
    picked_grad = back_grads.reshape(row_total, model_width)[slot_index].reshape(
        tok_count, chosen, model_width
    )
    input_grad = jnp.sum(picked_grad.astype(jnp.float32), axis=1).astype(jnp.bfloat16)
    up_gradient = lax.psum_scatter(
        contract_rows(expert_rows, up_grad).astype(jnp.bfloat16),
        "dp",
        scatter_dimension=0,
        tiled=True,
    ).astype(jnp.float32)
    down_gradient = lax.psum_scatter(
        contract_rows(hidden, grad_rows).astype(jnp.bfloat16), "dp", scatter_dimension=0, tiled=True
    ).astype(jnp.float32)
    up_new = adam_update(w_up_use[0], m_up_use[0], v_up_use[0], up_gradient)
    down_new = adam_update(w_down_use[0], m_down_use[0], v_down_use[0], down_gradient)
    return (
        mixed,
        input_grad,
        up_new[0][None],
        down_new[0][None],
        up_new[1][None],
        up_new[2][None],
        down_new[1][None],
        down_new[2][None],
    )


def solution(mesh):
    return jax.shard_map(
        body,
        mesh=mesh,
        in_specs=(
            P(("dp", "expert"), None),
            P(("dp", "expert"), None),
            P(("dp", "expert"), None),
            P(("dp", "expert"), None),
            P(),
            P("expert", "dp", None),
            P("expert", "dp", None),
            P("expert", "dp", None),
            P("expert", "dp", None),
            P("expert", "dp", None),
            P("expert", "dp", None),
        ),
        out_specs=(
            P(("dp", "expert"), None),
            P(("dp", "expert"), None),
            P("expert", "dp", None),
            P("expert", "dp", None),
            P("expert", "dp", None),
            P("expert", "dp", None),
            P("expert", "dp", None),
            P("expert", "dp", None),
        ),
        check_vma=False,
    )
```

profile of v0, /device:TPU:8, one launch (start us, length us, event | category | flops | bytes accessed | tf_op | source)
XLA Modules:
  0.0 443.3 jit_solution(2398692835408480219)
XLA Ops:
  14.7 4.3 fusion.38
  19.0 6.6 %collective-permute-done = bf16[1,256,1408]{2,1,0:T(8,128)(2,1)S(1)} collective-permute-done((bf16[1,256,1408]{2,1,0:T(8,128)(2,1)}, bf16[1,256,1408]{2,1,0:T(8,128)(2,1)S(1)}, u32[]{:S(2)}, u32[]{:S(2)}) %collective-permute-start) | collective-permute-done | bytes 720928 | tf_op jit(solution)/shard_map/ppermute | solution.py:16
  28.2 15.6 %fusion.42 = (s32[288]{0:T(512)S(1)}, s32[288]{0:T(512)S(1)}) fusion(s32[288]{0:T(512)S(1)} %reshape.168, pred[288]{0:T(512)(128)(4,1)S(1)} %get-tuple-element.32, pred[288]{0:T(512)(128)(4,1)S(1)} %get-tuple-element.31, pred[288]{0:T(512)(128)(4,1)S(1)} %get-tuple-element.30, pred[288]{0:T(512)(128)(4,1)S(1)} %get-tuple-element.29, ...), kind=kLoop, calls=%fused_computation.115 | loop fusion | flops 7488 | bytes 11908 | tf_op jit(solution)/shard_map/xor | solution.py:84
  51.2 3.1 gather_fusion.2
  54.3 3.2 gather_fusion
  59.9 3.9 reshape.180
  67.4 81.6 %all_to_all.15 = bf16[32,24,2048]{2,1,0:T(8,128)(2,1)S(1)} all-to-all(bf16[32,24,2048]{2,1,0:T(8,128)(2,1)S(1)} %pad_maximum_fusion), channel_id=1, replica_groups=mesh['dp'=8,'expert'=32] {'expert'}, dimensions={0} | all-to-all | bytes 6291456 | tf_op jit(solution)/shard_map/all_to_all | solution.py:109
  151.3 3.6 reshape.172
  156.3 5.8 %fusion.6 = f32[384,1408]{1,0:T(8,128)S(1)} fusion(bf16[384,2048]{1,0:T(8,128)(2,1)} %reshape.172, bf16[1,2048,1408]{2,1,0:T(8,128)(2,1)} %all-gather.3.cloned.1.call-done), kind=kOutput, calls=%fused_computation.14 | convolution fusion | flops 2214592512 | bytes 9502720 | tf_op jit(solution)/shard_map/dot_general | solution.py:118
  163.5 5.1 %convolution_convert_fusion = bf16[1408,2048]{1,0:T(8,128)(2,1)} fusion(bf16[384,2048]{1,0:T(8,128)(2,1)S(1)} %copy-done.9, f32[384,1408]{1,0:T(8,128)S(1)} %fusion.6), kind=kOutput, calls=%fused_computation.6 | convolution fusion | flops 2220179456 | bytes 9502720 | tf_op jit(solution)/shard_map/dot_general | solution.py:42
  174.0 43.8 %collective-permute-done.1 = bf16[1,176,2048]{2,1,0:T(8,128)(2,1)S(1)} collective-permute-done((bf16[1,176,2048]{2,1,0:T(8,128)(2,1)S(1)}, bf16[1,176,2048]{2,1,0:T(8,128)(2,1)S(1)}, u32[]{:S(2)}, u32[]{:S(2)}) %collective-permute-start.1) | collective-permute-done | bytes 720928 | tf_op jit(solution)/shard_map/ppermute | solution.py:16
  218.6 5.2 %fusion.35 = (bf16[1,176,2048]{2,1,0:T(8,128)(2,1)}, bf16[1,176,2048]{2,1,0:T(8,128)(2,1)}, bf16[1,176,2048]{2,1,0:T(8,128)(2,1)}, bf16[1,176,2048]{2,1,0:T(8,128)(2,1)}) fusion(bf16[176,2048]{1,0:T(8,128)(2,1)} %reduce-scatter.5.cloned.1.call-done, bf16[1,176,2048]{2,1,0:T(8,128)(2,1)S(1)} %copy-done.6, bf16[2,176,2048]{2,1,0:T(8,128)(2,1)} %collective-permute-done.3, ...), kind=kLoop, calls=%fused_computation.55 | loop fusion | flops 7929856 | bytes 7929857 | tf_op jit(solution)/shard_map/broadcast_in_dim | solution.py:161
  224.0 40.1 %all-gather.5.cloned.1.call-done = bf16[1,1408,2048]{2,1,0:T(8,128)(2,1)} async-done(((bf16[1,176,2048]{2,1,0:T(8,128)(2,1)}), bf16[1,1408,2048]{2,1,0:T(8,128)(2,1)}) %all-gather.5.cloned.1.call-update) | async-done | bytes 5767184 | tf_op jit(solution)/shard_map/all_gather | solution.py:108
  264.2 7.2 %fusion.11 = bf16[384,1408]{1,0:T(8,128)(2,1)S(1)} fusion(bf16[384,2048]{1,0:T(8,128)(2,1)S(1)} %copy-done.9, bf16[1,1408,2048]{2,1,0:T(8,128)(2,1)} %all-gather.5.cloned.1.call-done, f32[384,1408]{1,0:T(8,128)} %copy-done.15), kind=kOutput, calls=%fused_computation.20 | convolution fusion | flops 2219458560 | bytes 10584064 | tf_op jit(solution)/shard_map/dot_general | solution.py:48
  272.3 5.1 %convolution_convert_fusion.1 = bf16[2048,1408]{1,0:T(8,128)(2,1)} fusion(bf16[384,2048]{1,0:T(8,128)(2,1)S(1)} %copy-done.8, bf16[384,1408]{1,0:T(8,128)(2,1)S(1)} %fusion.11), kind=kOutput, calls=%fused_computation.7 | convolution fusion | flops 2217476096 | bytes 8421376 | tf_op jit(solution)/shard_map/dot_general | solution.py:42
  278.7 5.3 %fusion.14 = bf16[384,2048]{1,0:T(8,128)(2,1)S(1)} fusion(bf16[384,1408]{1,0:T(8,128)(2,1)S(1)} %copy-done.14, bf16[1,2048,1408]{2,1,0:T(8,128)(2,1)} %all-gather.3.cloned.1.call-done), kind=kOutput, calls=%fused_computation.21 | convolution fusion | flops 2215378944 | bytes 8421376 | tf_op jit(solution)/shard_map/dot_general | solution.py:48
  285.6 10.2 %all-to-all-start.2 = ((bf16[32,12,2048]{2,1,0:T(8,128)(2,1)}), bf16[32,12,2048]{2,1,0:T(8,128)(2,1)S(1)}, u32[]{:S(2)}, u32[]{:S(2)}) async-start(bf16[32,12,2048]{2,1,0:T(8,128)(2,1)} %reshape.176), calls=%async_computation.2 | async-start | bytes 4194304 | tf_op jit(solution)/shard_map/all_to_all | solution.py:135
  295.7 7.3 %fusion.17 = bf16[384,2048]{1,0:T(8,128)(2,1)} fusion(bf16[1,1408,2048]{2,1,0:T(8,128)(2,1)} %all-gather.5.cloned.1.call-done, f32[384,1408]{1,0:T(8,128)} %copy-done.15), kind=kOutput, calls=%fused_computation.22 | convolution fusion | flops 2218082304 | bytes 9502720 | tf_op jit(solution)/shard_map/dot_general | solution.py:120
  303.0 3.7 reshape.173
  306.6 37.0 %all-to-all-done.2 = bf16[32,12,2048]{2,1,0:T(8,128)(2,1)S(1)} async-done(((bf16[32,12,2048]{2,1,0:T(8,128)(2,1)}), bf16[32,12,2048]{2,1,0:T(8,128)(2,1)S(1)}, u32[]{:S(2)}, u32[]{:S(2)}) %all-to-all-start.2) | async-done | bytes 1572896 | tf_op jit(solution)/shard_map/all_to_all | solution.py:135
  345.0 9.0 %all-to-all-start.1 = ((bf16[32,12,2048]{2,1,0:T(8,128)(2,1)}), bf16[32,12,2048]{2,1,0:T(8,128)(2,1)}, u32[]{:S(2)}, u32[]{:S(2)}) async-start(bf16[32,12,2048]{2,1,0:T(8,128)(2,1)} %reshape.173), calls=%async_computation.1 | async-start | bytes 4194304 | tf_op jit(solution)/shard_map/all_to_all | solution.py:121
  364.1 40.4 %all-to-all-done.1 = bf16[32,12,2048]{2,1,0:T(8,128)(2,1)} async-done(((bf16[32,12,2048]{2,1,0:T(8,128)(2,1)}), bf16[32,12,2048]{2,1,0:T(8,128)(2,1)}, u32[]{:S(2)}, u32[]{:S(2)}) %all-to-all-start.1) | async-done | bytes 1572896 | tf_op jit(solution)/shard_map/all_to_all | solution.py:121
  417.1 14.6 %collective-permute-done.2 = bf16[2,256,1408]{2,1,0:T(8,128)(2,1)} collective-permute-done((bf16[2,256,1408]{2,1,0:T(8,128)(2,1)}, bf16[2,256,1408]{2,1,0:T(8,128)(2,1)}, u32[]{:S(2)}, u32[]{:S(2)}) %collective-permute-start.2) | collective-permute-done | bytes 1441824 | tf_op jit(solution)/shard_map/ppermute | solution.py:16
  431.6 5.2 %fusion.30 = (bf16[1,256,1408]{2,1,0:T(8,128)(2,1)}, bf16[1,256,1408]{2,1,0:T(8,128)(2,1)}, bf16[1,256,1408]{2,1,0:T(8,128)(2,1)}) fusion(bf16[256,1408]{1,0:T(8,128)(2,1)} %reduce-scatter.3.cloned.1.call-done, bf16[1,256,1408]{2,1,0:T(8,128)(2,1)} %param.19, bf16[2,256,1408]{2,1,0:T(8,128)(2,1)} %collective-permute-done.2, pred[]{:T(512)} %bitcast.33, ...), kind=kLoop, calls=%fused_computation.44 | loop fusion | flops 7569408 | bytes 6488065 | tf_op jit(solution)/shard_map/broadcast_in_dim | solution.py:163
  (92 shorter events, 62.1 us)
Async XLA Ops:
  7.2 44.0 %copy-start = (bf16[48,2048]{1,0:T(8,128)(2,1)S(1)}, bf16[48,2048]{1,0:T(8,128)(2,1)}, u32[]{:S(2)}) copy-start(bf16[48,2048]{1,0:T(8,128)(2,1)} %param.14) | copy-start | bytes 589828
  7.2 20.8 %copy-start.12 = (f32[48,6]{0,1:T(8,128)S(1)}, f32[48,6]{0,1:T(8,128)}, u32[]{:S(2)}) copy-start(f32[48,6]{0,1:T(8,128)} %param.13) | copy-start | bytes 3460
  7.2 149.1 %all-gather.3.cloned.1.call-start = ((), (), s32[]{:S(2)}) async-start(), calls=%async_computation.5 | async-start | bytes 6488064 | tf_op jit(solution)/shard_map/all_gather | solution.py:107
  7.2 18.4 %collective-permute-start = (bf16[1,256,1408]{2,1,0:T(8,128)(2,1)}, bf16[1,256,1408]{2,1,0:T(8,128)(2,1)S(1)}, u32[]{:S(2)}, u32[]{:S(2)}) collective-permute-start(bf16[1,256,1408]{2,1,0:T(8,128)(2,1)} %param.16), channel_id=1, source_target_pairs={{0,1},{1,0},{2,3},{3,2},{4,5},{5,4},{6,7},{7,6},{8,9},{9,8},{10,11... | collective-permute-start | bytes 2162696 | tf_op jit(solution)/shard_map/ppermute | solution.py:16
  27.7 190.9 %reduce-scatter.5.cloned.1.call-start = ((), (), s32[]{:S(2)}) async-start(), calls=%async_computation.8 | async-start | bytes 6488064 | tf_op jit(solution)/shard_map/reduce_scatter | solution.py:152
  51.2 3.1 copy-start.2
  63.8 2.2 copy-start.3
  156.3 7.2 %copy-start.9 = (bf16[384,2048]{1,0:T(8,128)(2,1)S(1)}, bf16[384,2048]{1,0:T(8,128)(2,1)}, u32[]{:S(2)}) copy-start(bf16[384,2048]{1,0:T(8,128)(2,1)} %reshape.175) | copy-start | bytes 4718596
  162.1 1.4 copy-start.15
  168.7 1.1 copy-start.6
  168.7 1.3 copy-start.7
  168.7 95.5 %all-gather.5.cloned.1.call-start = ((), (), s32[]{:S(2)}) async-start(), calls=%async_computation.6 | async-start | bytes 6488064 | tf_op jit(solution)/shard_map/all_gather | solution.py:108
  170.0 3.1 copy-start.10
  170.1 48.5 %collective-permute-start.3 = (bf16[2,176,2048]{2,1,0:T(8,128)(2,1)S(1)}, bf16[2,176,2048]{2,1,0:T(8,128)(2,1)}, u32[]{:S(2)}, u32[]{:S(2)}) collective-permute-start(bf16[2,176,2048]{2,1,0:T(8,128)(2,1)S(1)} %pad_maximum_fusion.2), channel_id=1, source_target_pairs={{0,1},{1,0},{2,3},{3,2},{4,5},{5,4},{6,7},{7,6},{8,9},{9,8},{10,11... | collective-permute-start | bytes 4325384 | tf_op jit(solution)/shard_map/ppermute | solution.py:16
  173.1 44.6 %collective-permute-start.1 = (bf16[1,176,2048]{2,1,0:T(8,128)(2,1)S(1)}, bf16[1,176,2048]{2,1,0:T(8,128)(2,1)S(1)}, u32[]{:S(2)}, u32[]{:S(2)}) collective-permute-start(bf16[1,176,2048]{2,1,0:T(8,128)(2,1)S(1)} %copy-done.10), channel_id=1, source_target_pairs={{0,1},{1,0},{2,3},{3,2},{4,5},{5,4},{6,7},{7,6},{8,9},{9,8},{10,11... | collective-permute-start | bytes 2162696 | tf_op jit(solution)/shard_map/ppermute | solution.py:16
  223.8 48.6 %copy-start.8 = (bf16[384,2048]{1,0:T(8,128)(2,1)S(1)}, bf16[384,2048]{1,0:T(8,128)(2,1)}, u32[]{:S(2)}) copy-start(bf16[384,2048]{1,0:T(8,128)(2,1)} %reshape.172) | copy-start | bytes 4718596
  223.8 207.8 %reduce-scatter.3.cloned.1.call-start = ((), (), s32[]{:S(2)}) async-start(), calls=%async_computation.7 | async-start | bytes 6488064 | tf_op jit(solution)/shard_map/reduce_scatter | solution.py:146
  277.5 1.2 copy-start.14
  285.6 58.1 %all-to-all-start.2 = ((bf16[32,12,2048]{2,1,0:T(8,128)(2,1)}), bf16[32,12,2048]{2,1,0:T(8,128)(2,1)S(1)}, u32[]{:S(2)}, u32[]{:S(2)}) async-start(bf16[32,12,2048]{2,1,0:T(8,128)(2,1)} %reshape.176), calls=%async_computation.2 | async-start | bytes 4194304 | tf_op jit(solution)/shard_map/all_to_all | solution.py:135
  306.6 47.3 %copy-start.5 = (bf16[1,256,1408]{2,1,0:T(8,128)(2,1)S(1)}, bf16[1,256,1408]{2,1,0:T(8,128)(2,1)}, u32[]{:S(2)}) copy-start(bf16[1,256,1408]{2,1,0:T(8,128)(2,1)} %param.19) | copy-start | bytes 2162692
  343.6 1.3 copy-start.4
  345.0 59.5 %all-to-all-start.1 = ((bf16[32,12,2048]{2,1,0:T(8,128)(2,1)}), bf16[32,12,2048]{2,1,0:T(8,128)(2,1)}, u32[]{:S(2)}, u32[]{:S(2)}) async-start(bf16[32,12,2048]{2,1,0:T(8,128)(2,1)} %reshape.173), calls=%async_computation.1 | async-start | bytes 4194304 | tf_op jit(solution)/shard_map/all_to_all | solution.py:121
  356.3 75.3 %collective-permute-start.2 = (bf16[2,256,1408]{2,1,0:T(8,128)(2,1)}, bf16[2,256,1408]{2,1,0:T(8,128)(2,1)}, u32[]{:S(2)}, u32[]{:S(2)}) collective-permute-start(bf16[2,256,1408]{2,1,0:T(8,128)(2,1)} %pad_maximum_fusion.1), channel_id=1, source_target_pairs={{0,1},{1,0},{2,3},{3,2},{4,5},{5,4},{6,7},{7,6},{8,9},{9,8},{10,11... | collective-permute-start | bytes 4325384 | tf_op jit(solution)/shard_map/ppermute | solution.py:16
  431.6 5.2 %copy-start.1 = (bf16[48,2048]{1,0:T(8,128)(2,1)S(1)}, bf16[48,2048]{1,0:T(8,128)(2,1)}, u32[]{:S(2)}) copy-start(bf16[48,2048]{1,0:T(8,128)(2,1)} %param.14) | copy-start | bytes 589828
  (2 other events, 1.9 us)
Sparse Core Ops, SparseCore 0:
  27.8 43.7 all-gather.2
  168.8 42.1 reduce-scatter.4
  223.9 40.2 all-gather.4
  277.6 44.1 reduce-scatter.2
where the time goes:
time: 445 us; the launch traced here: 443 us
  waiting for transfers between devices  182 us (41%)
  blocking collectives  81.6 us (18%)
  local copies, waits for them, and re-layouts  59.5 us (13%)
  other arithmetic  42.5 us (10%)
  matrix products  35.7 us (8%)
  starting transfers between devices  26.8 us (6%)
  between operations  14.7 us (3%)
    all_to_all x1, blocking collectives, body(): lax.all_to_all(jnp.concatenate([send_tokens, send_grads], axis=1), 'exper...  81.6 us
    ppermute x4, waiting for transfers between devices, partner(): return lax.ppermute(value, axis, pairs)  64.9 us
    all_to_all x1, waiting for transfers between devices, body(): lax.all_to_all(expert_out.reshape(experts, capacity, model_width), 'exper...  40.4 us
    all_gather x1, waiting for transfers between devices, body(): down_full = lax.all_gather(w_down_use, 'dp', axis=1, tiled=True)[0]  40.1 us
    all_to_all x1, waiting for transfers between devices, body(): lax.all_to_all(input_part.reshape(experts, capacity, model_width), 'exper...  37 us
    xor x1, other arithmetic, body(): dest_routes = jnp.bitwise_xor(flat_routes, swap_flag[flat_routes])  15.6 us
    dot_general x2, matrix products, contract_cols(): lax.dot_general(left, right, (((1,), (1,)), ((), ())), preferred_element_...  12.4 us
    dot_general x2, matrix products, contract_rows(): lax.dot_general(left, right, (((0,), (0,)), ((), ())), preferred_element_...  10.2 us
  transfers between devices with their start and end apart: 10, of which 6 were waited for; matrix products, arithmetic and copies ran while one was open for 21% of the time, Pallas kernels for 0%

commit v1 on v0

--- a/solution.py
+++ b/solution.py
@@ -105,7 +105,9 @@
         .reshape(experts, capacity, model_width)
     )
     up_full = lax.all_gather(w_up_use, "dp", axis=1, tiled=True)[0]
-    down_full = lax.all_gather(w_down_use, "dp", axis=1, tiled=True)[0]
+    down_full = jnp.concatenate(
+        lax.all_to_all(jnp.stack([w_down_use] * lax.axis_size("dp")), "dp", 0, 0), axis=1
+    )[0]
     got_both = lax.all_to_all(
         jnp.concatenate([send_tokens, send_grads], axis=1),
         "expert",

time: 445 us -> 466 us (1.047)
  blocking collectives: 81.6 us -> 153 us
  waiting for transfers between devices: 182 us -> 141 us
    all_to_all x0 -> x1, blocking collectives: none -> 71.6 us  [body(): lax.all_to_all(jnp.stack([w_down_use] * lax.axis_size('dp')), 'dp', 0, 0)]
    all_gather x1 -> x0, waiting for transfers between devices: 40.1 us -> none  [body(): down_full = lax.all_gather(w_down_use, 'dp', axis=1, tiled=True)[0]]
    unnamed x34 -> x38, local copies, waits for them, and re-layouts: 10 us -> 9.96 us
  transfers between devices with their start and end apart: 10 -> 9, of which waited for: 6 -> 5; matrix products, arithmetic and copies ran while one was open for 21% -> 20% of each run, Pallas kernels for 0% -> 0%
where the time goes in v1:
time: 466 us; the launch traced here: 464 us
  blocking collectives  153 us (33%)
  waiting for transfers between devices  141 us (30%)
  local copies, waits for them, and re-layouts  57.9 us (12%)
  other arithmetic  41.7 us (9%)
  matrix products  31.4 us (7%)
  starting transfers between devices  24.2 us (5%)
  between operations  14.7 us (3%)
    all_to_all x1, blocking collectives, body(): lax.all_to_all(jnp.concatenate([send_tokens, send_grads], axis=1), 'exper...  81.6 us
    all_to_all x1, blocking collectives, body(): lax.all_to_all(jnp.stack([w_down_use] * lax.axis_size('dp')), 'dp', 0, 0)  71.6 us
    ppermute x4, waiting for transfers between devices, partner(): return lax.ppermute(value, axis, pairs)  64.4 us
    all_to_all x1, waiting for transfers between devices, body(): lax.all_to_all(expert_out.reshape(experts, capacity, model_width), 'exper...  40.4 us
    all_to_all x1, waiting for transfers between devices, body(): lax.all_to_all(input_part.reshape(experts, capacity, model_width), 'exper...  36.2 us
    xor x1, other arithmetic, body(): dest_routes = jnp.bitwise_xor(flat_routes, swap_flag[flat_routes])  15.6 us
    dot_general x2, matrix products, contract_rows(): lax.dot_general(left, right, (((0,), (0,)), ((), ())), preferred_element_...  10.2 us
    unnamed x38, local copies, waits for them, and re-layouts  9.96 us
  transfers between devices with their start and end apart: 9, of which 5 were waited for; matrix products, arithmetic and copies ran while one was open for 20% of the time, Pallas kernels for 0%

profile of v1, /device:TPU:8, one launch (start us, length us, event | category | flops | bytes accessed | tf_op | source)
XLA Modules:
  0.0 464.4 jit_solution(4760176438642734340)
XLA Ops:
  14.7 4.3 fusion.25
  19.0 6.6 %collective-permute-done = bf16[1,256,1408]{2,1,0:T(8,128)(2,1)S(1)} collective-permute-done((bf16[1,256,1408]{2,1,0:T(8,128)(2,1)}, bf16[1,256,1408]{2,1,0:T(8,128)(2,1)S(1)}, u32[]{:S(2)}, u32[]{:S(2)}) %collective-permute-start) | collective-permute-done | bytes 720928 | tf_op jit(solution)/shard_map/ppermute | solution.py:16
  28.0 15.6 %fusion.29 = (s32[288]{0:T(512)S(1)}, s32[288]{0:T(512)S(1)}) fusion(s32[288]{0:T(512)S(1)} %reshape.169, pred[288]{0:T(512)(128)(4,1)S(1)} %get-tuple-element.32, pred[288]{0:T(512)(128)(4,1)S(1)} %get-tuple-element.31, pred[288]{0:T(512)(128)(4,1)S(1)} %get-tuple-element.30, pred[288]{0:T(512)(128)(4,1)S(1)} %get-tuple-element.29, ...), kind=kLoop, calls=%fused_computation.110 | loop fusion | flops 7488 | bytes 11908 | tf_op jit(solution)/shard_map/xor | solution.py:84
  55.7 3.1 gather_fusion
  65.0 81.6 %all_to_all.20 = bf16[32,24,2048]{2,1,0:T(8,128)(2,1)S(1)} all-to-all(bf16[32,24,2048]{2,1,0:T(8,128)(2,1)S(1)} %pad_maximum_fusion), channel_id=1, replica_groups=mesh['dp'=8,'expert'=32] {'expert'}, dimensions={0} | all-to-all | bytes 6291456 | tf_op jit(solution)/shard_map/all_to_all | solution.py:111
  148.9 3.6 reshape.173
  154.0 5.8 %fusion.2 = f32[384,1408]{1,0:T(8,128)S(1)} fusion(bf16[384,2048]{1,0:T(8,128)(2,1)} %reshape.173, bf16[1,2048,1408]{2,1,0:T(8,128)(2,1)} %all-gather.2.cloned.1.call-done), kind=kOutput, calls=%fused_computation.10 | convolution fusion | flops 2214592512 | bytes 9502720 | tf_op jit(solution)/shard_map/dot_general | solution.py:120
  161.2 5.1 %convolution_convert_fusion = bf16[1408,2048]{1,0:T(8,128)(2,1)} fusion(bf16[384,2048]{1,0:T(8,128)(2,1)S(1)} %copy-done.10, f32[384,1408]{1,0:T(8,128)S(1)} %fusion.2), kind=kOutput, calls=%fused_computation.6 | convolution fusion | flops 2220179456 | bytes 9502720 | tf_op jit(solution)/shard_map/dot_general | solution.py:42
  167.8 3.0 collective-permute-start.3
  171.6 43.8 %collective-permute-done.1 = bf16[1,176,2048]{2,1,0:T(8,128)(2,1)S(1)} collective-permute-done((bf16[1,176,2048]{2,1,0:T(8,128)(2,1)S(1)}, bf16[1,176,2048]{2,1,0:T(8,128)(2,1)S(1)}, u32[]{:S(2)}, u32[]{:S(2)}) %collective-permute-start.1) | collective-permute-done | bytes 720928 | tf_op jit(solution)/shard_map/ppermute | solution.py:16
  216.3 4.5 fusion.21
  221.5 71.6 %all_to_all.21 = bf16[8,1,176,2048]{3,2,1,0:T(8,128)(2,1)S(1)} all-to-all(bf16[8,1,176,2048]{3,2,1,0:T(8,128)(2,1)S(1)} %stack.2), channel_id=1, replica_groups=mesh['dp'=8,'expert'=32] {'dp'}, dimensions={0} | all-to-all | bytes 11534336 | tf_op jit(solution)/shard_map/all_to_all | solution.py:109
  297.0 5.1 %convolution_convert_fusion.1 = bf16[2048,1408]{1,0:T(8,128)(2,1)} fusion(bf16[384,2048]{1,0:T(8,128)(2,1)S(1)} %copy-done.9, bf16[384,1408]{1,0:T(8,128)(2,1)S(1)} %fusion.4), kind=kOutput, calls=%fused_computation.7 | convolution fusion | flops 2217476096 | bytes 8421376 | tf_op jit(solution)/shard_map/dot_general | solution.py:42
  303.3 5.3 %fusion.5 = bf16[384,2048]{1,0:T(8,128)(2,1)S(1)} fusion(bf16[384,1408]{1,0:T(8,128)(2,1)S(1)} %copy-done.15, bf16[1,2048,1408]{2,1,0:T(8,128)(2,1)} %all-gather.2.cloned.1.call-done), kind=kOutput, calls=%fused_computation.17 | convolution fusion | flops 2215378944 | bytes 8421376 | tf_op jit(solution)/shard_map/dot_general | solution.py:48
  310.2 8.1 %all-to-all-start.3 = ((bf16[32,12,2048]{2,1,0:T(8,128)(2,1)}), bf16[32,12,2048]{2,1,0:T(8,128)(2,1)S(1)}, u32[]{:S(2)}, u32[]{:S(2)}) async-start(bf16[32,12,2048]{2,1,0:T(8,128)(2,1)} %reshape.177), calls=%async_computation.3 | async-start | bytes 4194304 | tf_op jit(solution)/shard_map/all_to_all | solution.py:137
  318.3 7.3 %convolution_convert_fusion.2 = bf16[384,2048]{1,0:T(8,128)(2,1)} fusion(bf16[1408,2048]{1,0:T(8,128)(2,1)} %bitcast.123, f32[384,1408]{1,0:T(8,128)} %copy-done.16), kind=kOutput, calls=%fused_computation.18 | convolution fusion | flops 2218082304 | bytes 9502720 | tf_op jit(solution)/shard_map/dot_general | solution.py:122
  325.5 3.7 reshape.174
  329.2 36.2 %all-to-all-done.3 = bf16[32,12,2048]{2,1,0:T(8,128)(2,1)S(1)} async-done(((bf16[32,12,2048]{2,1,0:T(8,128)(2,1)}), bf16[32,12,2048]{2,1,0:T(8,128)(2,1)S(1)}, u32[]{:S(2)}, u32[]{:S(2)}) %all-to-all-start.3) | async-done | bytes 1572896 | tf_op jit(solution)/shard_map/all_to_all | solution.py:137
  366.8 8.7 %all-to-all-start.2 = ((bf16[32,12,2048]{2,1,0:T(8,128)(2,1)}), bf16[32,12,2048]{2,1,0:T(8,128)(2,1)}, u32[]{:S(2)}, u32[]{:S(2)}) async-start(bf16[32,12,2048]{2,1,0:T(8,128)(2,1)} %reshape.174), calls=%async_computation.2 | async-start | bytes 4194304 | tf_op jit(solution)/shard_map/all_to_all | solution.py:123
  385.6 40.4 %all-to-all-done.2 = bf16[32,12,2048]{2,1,0:T(8,128)(2,1)} async-done(((bf16[32,12,2048]{2,1,0:T(8,128)(2,1)}), bf16[32,12,2048]{2,1,0:T(8,128)(2,1)}, u32[]{:S(2)}, u32[]{:S(2)}) %all-to-all-start.2) | async-done | bytes 1572896 | tf_op jit(solution)/shard_map/all_to_all | solution.py:123
  428.5 3.0 gather_fusion.3
  433.6 3.1 reduce_sum.32
  438.5 14.1 %collective-permute-done.2 = bf16[2,256,1408]{2,1,0:T(8,128)(2,1)} collective-permute-done((bf16[2,256,1408]{2,1,0:T(8,128)(2,1)}, bf16[2,256,1408]{2,1,0:T(8,128)(2,1)}, u32[]{:S(2)}, u32[]{:S(2)}) %collective-permute-start.2) | collective-permute-done | bytes 1441824 | tf_op jit(solution)/shard_map/ppermute | solution.py:16
  452.6 5.2 %fusion.17 = (bf16[1,256,1408]{2,1,0:T(8,128)(2,1)}, bf16[1,256,1408]{2,1,0:T(8,128)(2,1)}, bf16[1,256,1408]{2,1,0:T(8,128)(2,1)}) fusion(bf16[256,1408]{1,0:T(8,128)(2,1)} %reduce-scatter.3.cloned.1.call-done, bf16[1,256,1408]{2,1,0:T(8,128)(2,1)} %param.19, bf16[2,256,1408]{2,1,0:T(8,128)(2,1)} %collective-permute-done.2, pred[]{:T(512)} %bitcast.33, ...), kind=kLoop, calls=%fused_computation.39 | loop fusion | flops 7569408 | bytes 6488065 | tf_op jit(solution)/shard_map/broadcast_in_dim | solution.py:165
  (95 shorter events, 61.0 us)
Async XLA Ops:
  7.2 40.7 %copy-start = (bf16[48,2048]{1,0:T(8,128)(2,1)S(1)}, bf16[48,2048]{1,0:T(8,128)(2,1)}, u32[]{:S(2)}) copy-start(bf16[48,2048]{1,0:T(8,128)(2,1)} %param.14) | copy-start | bytes 589828
  7.2 146.8 %all-gather.2.cloned.1.call-start = ((), (), s32[]{:S(2)}) async-start(), calls=%async_computation.6 | async-start | bytes 6488064 | tf_op jit(solution)/shard_map/all_gather | solution.py:107
  7.2 18.4 %collective-permute-start = (bf16[1,256,1408]{2,1,0:T(8,128)(2,1)}, bf16[1,256,1408]{2,1,0:T(8,128)(2,1)S(1)}, u32[]{:S(2)}, u32[]{:S(2)}) collective-permute-start(bf16[1,256,1408]{2,1,0:T(8,128)(2,1)} %param.16), channel_id=1, source_target_pairs={{0,1},{1,0},{2,3},{3,2},{4,5},{5,4},{6,7},{7,6},{8,9},{9,8},{10,11... | collective-permute-start | bytes 2162696 | tf_op jit(solution)/shard_map/ppermute | solution.py:16
  27.7 188.6 %reduce-scatter.5.cloned.1.call-start = ((), (), s32[]{:S(2)}) async-start(), calls=%async_computation.8 | async-start | bytes 6488064 | tf_op jit(solution)/shard_map/reduce_scatter | solution.py:154
  50.3 2.3 copy-start.13
  52.6 3.1 copy-start.2
  61.4 2.2 copy-start.3
  154.0 7.2 %copy-start.10 = (bf16[384,2048]{1,0:T(8,128)(2,1)S(1)}, bf16[384,2048]{1,0:T(8,128)(2,1)}, u32[]{:S(2)}) copy-start(bf16[384,2048]{1,0:T(8,128)(2,1)} %reshape.176) | copy-start | bytes 4718596
  159.8 1.4 copy-start.16
  166.3 1.3 copy-start.8
  166.3 286.3 %reduce-scatter.3.cloned.1.call-start = ((), (), s32[]{:S(2)}) async-start(), calls=%async_computation.7 | async-start | bytes 6488064 | tf_op jit(solution)/shard_map/reduce_scatter | solution.py:148
  167.6 3.1 copy-start.11
  167.8 48.5 %collective-permute-start.3 = (bf16[2,176,2048]{2,1,0:T(8,128)(2,1)S(1)}, bf16[2,176,2048]{2,1,0:T(8,128)(2,1)}, u32[]{:S(2)}, u32[]{:S(2)}) collective-permute-start(bf16[2,176,2048]{2,1,0:T(8,128)(2,1)S(1)} %pad_maximum_fusion.2), channel_id=1, source_target_pairs={{0,1},{1,0},{2,3},{3,2},{4,5},{5,4},{6,7},{7,6},{8,9},{9,8},{10,11... | collective-permute-start | bytes 4325384 | tf_op jit(solution)/shard_map/ppermute | solution.py:16
  170.8 44.6 %collective-permute-start.1 = (bf16[1,176,2048]{2,1,0:T(8,128)(2,1)S(1)}, bf16[1,176,2048]{2,1,0:T(8,128)(2,1)S(1)}, u32[]{:S(2)}, u32[]{:S(2)}) collective-permute-start(bf16[1,176,2048]{2,1,0:T(8,128)(2,1)S(1)} %copy-done.11), channel_id=1, source_target_pairs={{0,1},{1,0},{2,3},{3,2},{4,5},{5,4},{6,7},{7,6},{8,9},{9,8},{10,11... | collective-permute-start | bytes 2162696 | tf_op jit(solution)/shard_map/ppermute | solution.py:16
  221.4 71.6 %copy-start.17 = (f32[384,1408]{1,0:T(8,128)S(1)}, f32[384,1408]{1,0:T(8,128)}, u32[]{:S(2)}) copy-start(f32[384,1408]{1,0:T(8,128)} %copy-done.16) | copy-start | bytes 6488068
  293.1 2.9 copy-start.5
  293.1 3.9 copy-start.9
  302.1 1.2 copy-start.15
  310.2 55.2 %all-to-all-start.3 = ((bf16[32,12,2048]{2,1,0:T(8,128)(2,1)}), bf16[32,12,2048]{2,1,0:T(8,128)(2,1)S(1)}, u32[]{:S(2)}, u32[]{:S(2)}) async-start(bf16[32,12,2048]{2,1,0:T(8,128)(2,1)} %reshape.177), calls=%async_computation.3 | async-start | bytes 4194304 | tf_op jit(solution)/shard_map/all_to_all | solution.py:137
  329.2 46.3 %copy-start.6 = (bf16[1,256,1408]{2,1,0:T(8,128)(2,1)S(1)}, bf16[1,256,1408]{2,1,0:T(8,128)(2,1)}, u32[]{:S(2)}) copy-start(bf16[1,256,1408]{2,1,0:T(8,128)(2,1)} %param.19) | copy-start | bytes 2162692
  365.4 1.3 copy-start.4
  366.8 59.2 %all-to-all-start.2 = ((bf16[32,12,2048]{2,1,0:T(8,128)(2,1)}), bf16[32,12,2048]{2,1,0:T(8,128)(2,1)}, u32[]{:S(2)}, u32[]{:S(2)}) async-start(bf16[32,12,2048]{2,1,0:T(8,128)(2,1)} %reshape.174), calls=%async_computation.2 | async-start | bytes 4194304 | tf_op jit(solution)/shard_map/all_to_all | solution.py:123
  377.8 74.8 %collective-permute-start.2 = (bf16[2,256,1408]{2,1,0:T(8,128)(2,1)}, bf16[2,256,1408]{2,1,0:T(8,128)(2,1)}, u32[]{:S(2)}, u32[]{:S(2)}) collective-permute-start(bf16[2,256,1408]{2,1,0:T(8,128)(2,1)} %pad_maximum_fusion.1), channel_id=1, source_target_pairs={{0,1},{1,0},{2,3},{3,2},{4,5},{5,4},{6,7},{7,6},{8,9},{9,8},{10,11... | collective-permute-start | bytes 4325384 | tf_op jit(solution)/shard_map/ppermute | solution.py:16
  452.6 5.2 %copy-start.1 = (bf16[48,2048]{1,0:T(8,128)(2,1)S(1)}, bf16[48,2048]{1,0:T(8,128)(2,1)}, u32[]{:S(2)}) copy-start(bf16[48,2048]{1,0:T(8,128)(2,1)} %param.14) | copy-start | bytes 589828
  (3 other events, 3.0 us)
Sparse Core Ops, SparseCore 0:
  27.8 43.7 all-gather.1
  166.4 42.0 reduce-scatter.4
  302.2 41.3 reduce-scatter.2
